TPU v7x, 32 devices: a whole 2x2x4 slice. The times are simulated.
32 devices in a mesh: groups: 2 (over x), seq: 8 (over z, y), rep: 2 (over core).
Axes of the slice: x: 2, y: 2, z: 4, core: 2. Of those that a mesh axis runs over, the one named last changes fastest.
Arguments:
- inputs: bfloat16 [4, 4096, 1536], P(('groups', 'rep'), 'seq'), parts along dimension 0, may hold values from -6 to 6
- lengths: int32 [4], P(('groups', 'rep')), parts along dimension 0, may hold values from 2049 to 4096, as said below
- conv_weight: bfloat16 [3, 48, 1536], replicated, may hold values from -0.5 to 0.5
- point_weight: bfloat16 [1536, 1536], replicated, may hold values from -0.15625 to 0.15625
- cotangent: bfloat16 [4, 4096, 1536], P(('groups', 'rep'), 'seq'), parts along dimension 0, may hold values from -6 to 6
Outputs:
- output: bfloat16 [4, 4096, 1536], P(('groups', 'rep'), 'seq'), parts along dimension 0
- grad_inputs: bfloat16 [4, 4096, 1536], P(('groups', 'rep'), 'seq'), parts along dimension 0
- grad_point: float32 [3072, 1536], P(('groups', 'seq', 'rep')), parts along dimension 0
- grad_conv: float32 [6, 48, 1536], P('groups'), parts along dimension 0
There are 2 independent parts, one for each index of `groups`. A program takes and returns all parts, laid end to end along the dimension named above; an argument that names none is the same for every part. Nothing has to cross between parts.
Inputs may be any that keep to these rules, and one draw needn't show every extreme that they name: `lengths`: one sample in each draw has all 4096 bins valid.
All inputs are finite; a program needn't handle non-finite values.
Results may differ from a plain program's by a relative error of at most 0.0031.
Values may be sent and summed in bfloat16 or wider, within the bound.
No kernel may reach another device: no remote copies, remote signals or barrier semaphores. Data moves between devices by JAX's collectives and lax.ppermute only.
A program may use at most 128 MiB of HBM per device.

v0:
```python
import math
import jax
import jax.numpy as jnp
from jax import lax
from jax.sharding import PartitionSpec as P

GROUP_CHANNELS = 48
DILATION_STEP = 64


def with_halo(cells, sides, width):
    for axis, dim in sides:
        count = lax.axis_size(axis)
        ends = count - 1
        head = lax.slice_in_dim(cells, 0, width, axis=dim)
        tail = lax.slice_in_dim(cells, cells.shape[dim] - width, cells.shape[dim], axis=dim)
        cells = jnp.concatenate(
            [
                lax.ppermute(tail, axis, [(i, (i + 1) % count) for i in range(ends)]),
                cells,
                lax.ppermute(head, axis, [((i + 1) % count, i) for i in range(ends)]),
            ],
            axis=dim,
        )
    return cells


def gelu_pair(pre):
    cdf = 0.5 * (1.0 + jax.scipy.special.erf(pre * 0.7071067811865476))
    dens = jnp.exp(-0.5 * pre * pre) * 0.3989422804014327
    return (pre * cdf, cdf + pre * dens)


def conv_taps(padded_input, weight, sequence_length):
    group_count = weight.shape[2] // GROUP_CHANNELS
    total = jnp.zeros(
        (padded_input.shape[0], sequence_length, group_count, GROUP_CHANNELS), jnp.float32
    )
    for kernel_offset in range(3):
        segment_window = padded_input[
            :, kernel_offset * DILATION_STEP : kernel_offset * DILATION_STEP + sequence_length
        ].reshape(padded_input.shape[0], sequence_length, group_count, GROUP_CHANNELS)
        wk = weight[kernel_offset].reshape(GROUP_CHANNELS, group_count, GROUP_CHANNELS)
        total = total + jnp.einsum(
            "slgi,igj->slgj", segment_window, wk, preferred_element_type=jnp.float32
        )
    return total.reshape(padded_input.shape[0], sequence_length, group_count * GROUP_CHANNELS)


def transpose_taps(padded_input, weight, sequence_length):
    group_count = weight.shape[2] // GROUP_CHANNELS
    total = jnp.zeros(
        (padded_input.shape[0], sequence_length, group_count, GROUP_CHANNELS), jnp.float32
    )
    for kernel_offset in range(3):
        segment_window = padded_input[
            :,
            (2 - kernel_offset) * DILATION_STEP : (2 - kernel_offset) * DILATION_STEP
            + sequence_length,
        ].reshape(padded_input.shape[0], sequence_length, group_count, GROUP_CHANNELS)
        wk = weight[kernel_offset].reshape(GROUP_CHANNELS, group_count, GROUP_CHANNELS)
        total = total + jnp.einsum(
            "slgj,igj->slgi", segment_window, wk, preferred_element_type=jnp.float32
        )
    return total.reshape(padded_input.shape[0], sequence_length, group_count * GROUP_CHANNELS)


def weight_taps(input_padded, output_gradient, sequence_length):
    group_count = output_gradient.shape[2] // GROUP_CHANNELS
    grouped = output_gradient.reshape(
        output_gradient.shape[0], sequence_length, group_count, GROUP_CHANNELS
    )
    taps = []
    for kernel_offset in range(3):
        segment_window = input_padded[
            :, kernel_offset * DILATION_STEP : kernel_offset * DILATION_STEP + sequence_length
        ].reshape(output_gradient.shape[0], sequence_length, group_count, GROUP_CHANNELS)
        taps.append(
            jnp.einsum(
                "slgi,slgj->igj", segment_window, grouped, preferred_element_type=jnp.float32
            ).reshape(GROUP_CHANNELS, group_count * GROUP_CHANNELS)
        )
    return jnp.stack(taps)


def on_device(inputs, lengths, conv_weight, point_weight, cotangent):
    local_bins = inputs.shape[1]
    chans = inputs.shape[2]
    seq_count = lax.axis_size("seq")
    rep_count = lax.axis_size("rep")
    seq_index = lax.axis_index("seq")
    positions = seq_index * local_bins + jnp.arange(local_bins, dtype=jnp.int32)
    mask = (positions[None, :] < lengths[:, None]).astype(jnp.float32)
    mask3 = mask[:, :, None]
    masked_input = (inputs.astype(jnp.float32) * mask3).astype(jnp.bfloat16)
    scale = 1.0 / math.sqrt(rep_count * seq_count * local_bins)
    padded_input = with_halo(masked_input, (("seq", 1),), DILATION_STEP)
    pre = conv_taps(padded_input, conv_weight, local_bins)
    act_val, slope = gelu_pair(pre)
    act = (act_val * mask3).astype(jnp.bfloat16)
    act_rows = act.reshape(local_bins, chans)
    cot_rows = cotangent.reshape(local_bins, chans)
    proj = jnp.dot(act_rows, point_weight, preferred_element_type=jnp.float32).reshape(inputs.shape)
    output = (inputs.astype(jnp.float32) + proj).astype(jnp.bfloat16)
    back = lax.dot_general(
        cot_rows, point_weight, (((1,), (1,)), ((), ())), preferred_element_type=jnp.float32
    )
    preactivation_gradient = (back.reshape(inputs.shape) * slope * mask3).astype(jnp.bfloat16)
    padded_gradient = with_halo(preactivation_gradient, (("seq", 1),), DILATION_STEP)
    spread = transpose_taps(padded_gradient, conv_weight, local_bins)
    conv_local = weight_taps(padded_input, preactivation_gradient, local_bins)
    grad_conv = lax.psum(conv_local, ("seq", "rep")) * scale
    grad_inputs = (cotangent.astype(jnp.float32) + mask3 * spread).astype(jnp.bfloat16)
    grad_point = lax.psum_scatter(
        lax.dot_general(
            act_rows, cot_rows, (((0,), (0,)), ((), ())), preferred_element_type=jnp.float32
        ),
        ("seq", "rep"),
        scatter_dimension=0,
        tiled=True,
    )
    grad_point = grad_point * scale
    return (output, grad_inputs, grad_point, grad_conv)


def solution(mesh):
    return jax.shard_map(
        on_device,
        mesh=mesh,
        in_specs=(
            P(("groups", "rep"), "seq", None),
            P(("groups", "rep")),
            P(),
            P(),
            P(("groups", "rep"), "seq", None),
        ),
        out_specs=(
            P(("groups", "rep"), "seq", None),
            P(("groups", "rep"), "seq", None),
            P(("groups", "seq", "rep"), None),
            P("groups", None, None),
        ),
        check_vma=False,
    )
```

profile of v0, /device:TPU:0, one launch (start us, length us, event | category | flops | bytes accessed | tf_op | source)
XLA Modules:
  0.0 282.3 jit_solution(17731582967760469702)
XLA Ops:
  7.9 1.7 fusion.1
  11.7 6.2 %collective-permute-start = (bf16[1,64,1536]{2,1,0:T(8,128)(2,1)}, bf16[1,64,1536]{2,1,0:T(8,128)(2,1)}, u32[]{:S(2)}, u32[]{:S(2)}) collective-permute-start(bf16[1,64,1536]{2,1,0:T(8,128)(2,1)} %get-tuple-element.11), channel_id=1, source_target_pairs={{0,2},{2,4},{4,6},{6,8},{8,10},{10,12},{12,14},{1,3},{3,5},{5,7},{... | collective-permute-start | bytes 589832 | tf_op jit(solution)/shard_map/ppermute | solution.py:19
  18.6 1.8 fusion.22
  21.5 1.8 copy.35
  23.3 1.8 copy.37
  25.2 3.2 %fusion.29 = f32[32,512,48]{1,2,0:T(8,128)} fusion(bf16[48,32,48]{0,2,1:T(8,128)(2,1)} %bitcast.90, bf16[512,32,48]{0,2,1:T(8,128)(2,1)S(1)} %bitcast.73), kind=kOutput, calls=%fused_computation.48 | convolution fusion | flops 75497472 | bytes 4866048 | tf_op jit(solution)/shard_map/slgi,igj->slgj/dot_general | solution.py:44
  28.4 2.9 %pad_maximum_fusion.2 = (bf16[1,512,1536]{2,1,0:T(8,128)(2,1)}, bf16[1,512,1536]{2,1,0:T(8,128)(2,1)}) fusion(bf16[1,64,1536]{2,1,0:T(8,128)(2,1)} %collective-permute-done.1, bf16[1,512,1536]{2,1,0:T(8,128)(2,1)S(1)} %fusion.1, bf16[1,64,1536]{2,1,0:T(8,128)(2,1)} %collective-permute-done), kind=kLoop, calls=%fused_computation.21 | loop fusion | flops 6291456 | bytes 5111808 | tf_op jit(solution)/shard_map/concatenate | solution.py:17
  31.3 2.6 copy.38
  33.9 1.7 copy.34
  35.7 2.0 fusion.28
  38.7 2.2 add_add_fusion.1
  40.9 3.7 %copy.41 = f32[512,1536]{1,0:T(8,128)} copy(f32[512,1536]{0,1:T(8,128)} %bitcast.79) | data formatting | bytes 6291456 | tf_op jit(solution)/shard_map/reshape | solution.py:47
  44.6 7.0 %fusion.7 = bf16[512,1536]{1,0:T(8,128)(2,1)} fusion(f32[512,1536]{1,0:T(8,128)} %copy.41, bf16[1536,1536]{1,0:T(8,128)(2,1)} %param.8, bf16[1,512,1536]{2,1,0:T(8,128)(2,1)S(1)} %copy-done.10, f32[512]{0:T(512)S(1)} %fusion.16), kind=kOutput, calls=%fused_computation.18 | convolution fusion | flops 2424569856 | bytes 11012096 | tf_op jit(solution)/shard_map/dot_general | solution.py:105
  51.5 1.7 copy.47
  53.3 3.0 %fusion.27 = f32[32,48,48]{2,1,0:T(8,128)} fusion(bf16[512,32,48]{0,2,1:T(8,128)(2,1)S(1)} %bitcast.69, bf16[512,32,48]{0,2,1:T(8,128)(2,1)} %bitcast.77), kind=kOutput, calls=%fused_computation.46 | convolution fusion | flops 75497472 | bytes 3440640 | tf_op jit(solution)/shard_map/slgi,slgj->igj/dot_general | solution.py:79
  57.7 1.5 fusion.25
  59.1 2.1 copy.52
  62.4 2.0 pad_maximum_fusion.4
  64.5 8.6 %fusion.8 = f32[1536,1536]{1,0:T(8,128)} fusion(bf16[1,512,1536]{2,1,0:T(8,128)(2,1)} %param.9, f32[1,512,1,1,1,1,1536]{1,6,5,4,3,2,0:T(8,128)} %bitcast.80, f32[512]{0:T(512)S(1)} %fusion.16), kind=kOutput, calls=%fused_computation.23 | convolution fusion | flops 2420637696 | bytes 14157824 | tf_op jit(solution)/shard_map/dot_general | solution.py:115
  74.6 4.2 %collective-permute-start.3 = (bf16[1,64,1536]{2,1,0:T(8,128)(2,1)S(1)}, bf16[1,64,1536]{2,1,0:T(8,128)(2,1)S(1)}, u32[]{:S(2)}, u32[]{:S(2)}) collective-permute-start(bf16[1,64,1536]{2,1,0:T(8,128)(2,1)S(1)} %get-tuple-element.6), channel_id=1, source_target_pairs={{0,2},{2,4},{4,6},{6,8},{8,10},{10,12},{12,14},{1,3},{3,5},{5,7},{... | collective-permute-start | bytes 589832 | tf_op jit(solution)/shard_map/ppermute | solution.py:19
  78.8 1.6 collective-permute-start.2
  80.4 7.6 %fusion.2 = bf16[1,512,1536]{2,1,0:T(8,128)(2,1)} fusion(bf16[1,512,1536]{2,1,0:T(8,128)(2,1)} %param.5, bf16[1536,1536]{1,0:T(8,128)(2,1)} %param.8, f32[512,1536]{1,0:T(8,128)} %copy.41, f32[512]{0:T(512)S(1)} %fusion.16), kind=kOutput, calls=%fused_computation.7 | convolution fusion | flops 2422996992 | bytes 11012096 | tf_op jit(solution)/shard_map/dot_general | solution.py:103
  88.0 2.3 fusion.24
  91.7 2.6 copy.49
  95.0 1.8 fusion.23
  97.5 2.3 add_add_fusion
  99.8 2.4 copy.51
  102.1 3.0 %add_convert_fusion = bf16[1,512,1536]{2,1,0:T(8,128)(2,1)} fusion(f32[1,512,1536]{2,1,0:T(8,128)S(1)} %copy.51, bf16[1,512,1536]{2,1,0:T(8,128)(2,1)} %param.9, f32[512]{0:T(512)S(1)} %fusion.16), kind=kLoop, calls=%fused_computation.13 | loop fusion | flops 3145728 | bytes 6293504 | tf_op jit(solution)/shard_map/convert_element_type | solution.py:113
  105.1 53.9 %all-reduce.2.cloned.1.call-done = f32[3,48,1536]{2,1,0:T(8,128)} async-done(((f32[3,48,1536]{2,1,0:T(8,128)}), f32[3,48,1536]{2,1,0:T(8,128)}) %all-reduce.2.cloned.1.call-update) | async-done | bytes 884752 | tf_op jit(solution)/shard_map/psum | solution.py:112
  159.1 2.2 broadcast_multiply_fusion
  161.2 112.3 %reduce-scatter.2.cloned.1.call-done = f32[96,1536]{1,0:T(8,128)} async-done(((f32[1536,1536]{1,0:T(8,128)}), f32[96,1536]{1,0:T(8,128)}) %reduce-scatter.2.cloned.1.call-update) | async-done | bytes 589840 | tf_op jit(solution)/shard_map/reduce_scatter | solution.py:114
  273.5 1.9 broadcast_multiply_fusion.1
  (41 shorter events, 11.9 us)
Async XLA Ops:
  7.2 151.9 %all-reduce.2.cloned.1.call-start = ((), (), s32[]{:S(2)}) async-start(), calls=%async_computation.2 | async-start | bytes 1769472 | tf_op jit(solution)/shard_map/psum | solution.py:112
  10.4 18.0 %collective-permute-start.1 = (bf16[1,64,1536]{2,1,0:T(8,128)(2,1)}, bf16[1,64,1536]{2,1,0:T(8,128)(2,1)}, u32[]{:S(2)}, u32[]{:S(2)}) collective-permute-start(bf16[1,64,1536]{2,1,0:T(8,128)(2,1)} %get-tuple-element.10), channel_id=1, source_target_pairs={{2,0},{4,2},{6,4},{8,6},{10,8},{12,10},{14,12},{3,1},{5,3},{7,5},{... | collective-permute-start | bytes 589832 | tf_op jit(solution)/shard_map/ppermute | solution.py:21
  11.7 16.7 %collective-permute-start = (bf16[1,64,1536]{2,1,0:T(8,128)(2,1)}, bf16[1,64,1536]{2,1,0:T(8,128)(2,1)}, u32[]{:S(2)}, u32[]{:S(2)}) collective-permute-start(bf16[1,64,1536]{2,1,0:T(8,128)(2,1)} %get-tuple-element.11), channel_id=1, source_target_pairs={{0,2},{2,4},{4,6},{6,8},{8,10},{10,12},{12,14},{1,3},{3,5},{5,7},{... | collective-permute-start | bytes 589832 | tf_op jit(solution)/shard_map/ppermute | solution.py:19
  35.6 5.3 %copy-start = (bf16[1,512,1536]{1,2,0:T(8,128)(2,1)}, bf16[1,512,1536]{1,2,0:T(8,128)(2,1)S(1)}, u32[]{:S(2)}) copy-start(bf16[1,512,1536]{1,2,0:T(8,128)(2,1)S(1)} %copy.34) | copy-start | bytes 4718596
  35.6 2.1 copy-start.2
  35.6 3.0 %copy-start.4 = (f32[32,512,48]{1,2,0:T(8,128)S(1)}, f32[32,512,48]{1,2,0:T(8,128)}, u32[]{:S(2)}) copy-start(f32[32,512,48]{1,2,0:T(8,128)} %fusion.29) | copy-start | bytes 9437188
  40.9 3.7 %copy-start.10 = (bf16[1,512,1536]{2,1,0:T(8,128)(2,1)S(1)}, bf16[1,512,1536]{2,1,0:T(8,128)(2,1)}, u32[]{:S(2)}) copy-start(bf16[1,512,1536]{2,1,0:T(8,128)(2,1)} %param.9) | copy-start | bytes 4718596
  53.3 4.4 %copy-start.1 = (bf16[1,512,1536]{1,2,0:T(8,128)(2,1)S(1)}, bf16[1,512,1536]{1,2,0:T(8,128)(2,1)}, u32[]{:S(2)}) copy-start(bf16[1,512,1536]{1,2,0:T(8,128)(2,1)} %copy-done) | copy-start | bytes 4718596
  57.7 3.5 %copy-start.9 = (f32[32,48,48]{2,1,0:T(8,128)S(1)}, f32[32,48,48]{2,1,0:T(8,128)}, u32[]{:S(2)}) copy-start(f32[32,48,48]{2,1,0:T(8,128)} %fusion.26) | copy-start | bytes 884740
  57.7 4.5 %copy-start.8 = (f32[32,48,48]{2,1,0:T(8,128)S(1)}, f32[32,48,48]{2,1,0:T(8,128)}, u32[]{:S(2)}) copy-start(f32[32,48,48]{2,1,0:T(8,128)} %fusion.27) | copy-start | bytes 884740
  64.5 209.1 %reduce-scatter.2.cloned.1.call-start = ((), (), s32[]{:S(2)}) async-start(), calls=%async_computation.1 | async-start | bytes 10027008 | tf_op jit(solution)/shard_map/reduce_scatter | solution.py:114
  73.2 1.4 copy-start.5
  74.6 15.7 %collective-permute-start.3 = (bf16[1,64,1536]{2,1,0:T(8,128)(2,1)S(1)}, bf16[1,64,1536]{2,1,0:T(8,128)(2,1)S(1)}, u32[]{:S(2)}, u32[]{:S(2)}) collective-permute-start(bf16[1,64,1536]{2,1,0:T(8,128)(2,1)S(1)} %get-tuple-element.6), channel_id=1, source_target_pairs={{0,2},{2,4},{4,6},{6,8},{8,10},{10,12},{12,14},{1,3},{3,5},{5,7},{... | collective-permute-start | bytes 589832 | tf_op jit(solution)/shard_map/ppermute | solution.py:19
  78.8 9.2 %copy-start.7 = (bf16[1,48,1536]{1,2,0:T(8,128)(2,1)S(1)}, bf16[1,48,1536]{1,2,0:T(8,128)(2,1)}, u32[]{:S(2)}) copy-start(bf16[1,48,1536]{1,2,0:T(8,128)(2,1)} %copy.37) | copy-start | bytes 442372
  78.8 11.5 %collective-permute-start.2 = (bf16[1,64,1536]{2,1,0:T(8,128)(2,1)S(1)}, bf16[1,64,1536]{2,1,0:T(8,128)(2,1)S(1)}, u32[]{:S(2)}, u32[]{:S(2)}) collective-permute-start(bf16[1,64,1536]{2,1,0:T(8,128)(2,1)S(1)} %get-tuple-element.7), channel_id=1, source_target_pairs={{2,0},{4,2},{6,4},{8,6},{10,8},{12,10},{14,12},{3,1},{5,3},{7,5},{... | collective-permute-start | bytes 589832 | tf_op jit(solution)/shard_map/ppermute | solution.py:21
  95.0 2.0 copy-start.3
  95.0 2.5 copy-start.6
Sparse Core Ops, SparseCore 0:
  64.6 94.4 all-reduce.1
  163.2 110.3 reduce-scatter.1
where the time goes:
time: 283 us; the launch traced here: 282 us
  waiting for transfers between devices  166 us (59%)
  matrix products  42.8 us (15%)
  local copies, waits for them, and re-layouts  29.9 us (11%)
  other arithmetic  15.1 us (5%)
  between operations  14.9 us (5%)
  starting transfers between devices  13.3 us (5%)
    reduce_scatter x1, waiting for transfers between devices, on_device(): lax.psum_scatter(lax.dot_general(act_rows, cot_rows, (((0,), (0,)), ((),...  112 us
    psum x1, waiting for transfers between devices, on_device(): grad_conv = lax.psum(conv_local, ('seq', 'rep')) * scale  53.9 us
    ppermute x2, starting transfers between devices, with_halo(): lax.ppermute(tail, axis, [(i, (i + 1) % count) for i in range(ends)])  10.4 us
    dot_general x1, matrix products, on_device(): lax.dot_general(act_rows, cot_rows, (((0,), (0,)), ((), ())), preferred_e...  8.65 us
    dot_general x1, matrix products, on_device(): jnp.dot(act_rows, point_weight, preferred_element_type=jnp.float32)  7.61 us
    dot_general x3, matrix products, conv_taps(): jnp.einsum('slgi,igj->slgj', segment_window, wk, preferred_element_type=j...  7.38 us
    dot_general x1, matrix products, on_device(): lax.dot_general(cot_rows, point_weight, (((1,), (1,)), ((), ())), preferr...  6.98 us
    slice x4, local copies, waits for them, and re-layouts, conv_taps(): weight[kernel_offset].reshape(GROUP_CHANNELS, group_count, GROUP_CHANNELS)  6.61 us
  transfers between devices with their start and end apart: 6, of which 2 were waited for; matrix products, arithmetic and copies ran while one was open for 16% of the time, Pallas kernels for 0%

commit v1 on v0

--- a/solution.py
+++ b/solution.py
@@ -3,6 +3,7 @@
 import jax.numpy as jnp
 from jax import lax
 from jax.sharding import PartitionSpec as P
+from jax.lax import psum
 
 GROUP_CHANNELS = 48
 DILATION_STEP = 64
@@ -109,7 +110,7 @@
     padded_gradient = with_halo(preactivation_gradient, (("seq", 1),), DILATION_STEP)
     spread = transpose_taps(padded_gradient, conv_weight, local_bins)
     conv_local = weight_taps(padded_input, preactivation_gradient, local_bins)
-    grad_conv = lax.psum(conv_local, ("seq", "rep")) * scale
+    grad_conv = psum(psum(conv_local, axis_name="rep"), "seq") * scale
     grad_inputs = (cotangent.astype(jnp.float32) + mask3 * spread).astype(jnp.bfloat16)
     grad_point = lax.psum_scatter(
         lax.dot_general(

time: 283 us -> 222 us (0.78)
  waiting for transfers between devices: 166 us -> 102 us
    reduce_scatter x1, waiting for transfers between devices: 112 us -> 10.3 us  [on_device(): lax.psum_scatter(lax.dot_general(act_rows, cot_rows, (((0,), (0,)), ((),...]
    psum x1 -> x2, waiting for transfers between devices: 53.9 us -> 92 us  [on_device(): grad_conv = psum(psum(conv_local, axis_name='rep'), 'seq') * scale]
  transfers between devices with their start and end apart: 6 -> 7, of which waited for: 2 -> 3; matrix products, arithmetic and copies ran while one was open for 16% -> 21% of each run, Pallas kernels for 0% -> 0%
where the time goes in v1:
time: 222 us; the launch traced here: 221 us
  waiting for transfers between devices  102 us (46%)
  matrix products  43.2 us (19%)
  local copies, waits for them, and re-layouts  31.1 us (14%)
  between operations  16.3 us (7%)
  other arithmetic  15.4 us (7%)
  starting transfers between devices  12.9 us (6%)
    psum x2, waiting for transfers between devices, on_device(): grad_conv = psum(psum(conv_local, axis_name='rep'), 'seq') * scale  92 us
    reduce_scatter x1, waiting for transfers between devices, on_device(): lax.psum_scatter(lax.dot_general(act_rows, cot_rows, (((0,), (0,)), ((),...  10.3 us
    ppermute x2, starting transfers between devices, with_halo(): lax.ppermute(tail, axis, [(i, (i + 1) % count) for i in range(ends)])  9.85 us
    dot_general x1, matrix products, on_device(): jnp.dot(act_rows, point_weight, preferred_element_type=jnp.float32)  8.41 us
    dot_general x1, matrix products, on_device(): lax.dot_general(act_rows, cot_rows, (((0,), (0,)), ((), ())), preferred_e...  8.21 us
    dot_general x3, matrix products, conv_taps(): jnp.einsum('slgi,igj->slgj', segment_window, wk, preferred_element_type=j...  7.37 us
    dot_general x1, matrix products, on_device(): lax.dot_general(cot_rows, point_weight, (((1,), (1,)), ((), ())), preferr...  6.99 us
    slice x4, local copies, waits for them, and re-layouts, conv_taps(): weight[kernel_offset].reshape(GROUP_CHANNELS, group_count, GROUP_CHANNELS)  6.62 us
  transfers between devices with their start and end apart: 7, of which 3 were waited for; matrix products, arithmetic and copies ran while one was open for 21% of the time, Pallas kernels for 0%

profile of v1, /device:TPU:0, one launch (start us, length us, event | category | flops | bytes accessed | tf_op | source)
XLA Modules:
  0.0 221.2 jit_solution(1034440676623830432)
XLA Ops:
  8.7 1.7 fusion.1
  12.5 6.2 %collective-permute-start = (bf16[1,64,1536]{2,1,0:T(8,128)(2,1)}, bf16[1,64,1536]{2,1,0:T(8,128)(2,1)}, u32[]{:S(2)}, u32[]{:S(2)}) collective-permute-start(bf16[1,64,1536]{2,1,0:T(8,128)(2,1)} %get-tuple-element.11), channel_id=1, source_target_pairs={{0,2},{2,4},{4,6},{6,8},{8,10},{10,12},{12,14},{1,3},{3,5},{5,7},{... | collective-permute-start | bytes 589832 | tf_op jit(solution)/shard_map/ppermute | solution.py:20
  19.4 1.8 fusion.22
  22.3 1.8 copy.35
  24.2 1.8 copy.37
  26.0 3.2 %fusion.29 = f32[32,512,48]{1,2,0:T(8,128)} fusion(bf16[48,32,48]{0,2,1:T(8,128)(2,1)} %bitcast.90, bf16[512,32,48]{0,2,1:T(8,128)(2,1)S(1)} %bitcast.73), kind=kOutput, calls=%fused_computation.48 | convolution fusion | flops 75497472 | bytes 4866048 | tf_op jit(solution)/shard_map/slgi,igj->slgj/dot_general | solution.py:45
  29.2 2.9 %pad_maximum_fusion.2 = (bf16[1,512,1536]{2,1,0:T(8,128)(2,1)}, bf16[1,512,1536]{2,1,0:T(8,128)(2,1)}) fusion(bf16[1,64,1536]{2,1,0:T(8,128)(2,1)} %collective-permute-done.1, bf16[1,512,1536]{2,1,0:T(8,128)(2,1)S(1)} %fusion.1, bf16[1,64,1536]{2,1,0:T(8,128)(2,1)} %collective-permute-done), kind=kLoop, calls=%fused_computation.21 | loop fusion | flops 6291456 | bytes 5111808 | tf_op jit(solution)/shard_map/concatenate | solution.py:18
  32.1 2.6 %copy.38 = bf16[1,512,1536]{1,2,0:T(8,128)(2,1)} copy(bf16[1,512,1536]{2,1,0:T(8,128)(2,1)} %get-tuple-element.8) | data formatting | bytes 3145728 | tf_op jit(solution)/shard_map/slice | solution.py:41
  34.7 1.7 copy.34
  36.5 2.0 fusion.28
  39.5 2.2 add_add_fusion.1
  41.7 3.7 %copy.41 = f32[512,1536]{1,0:T(8,128)} copy(f32[512,1536]{0,1:T(8,128)} %bitcast.79) | data formatting | bytes 6291456 | tf_op jit(solution)/shard_map/reshape | solution.py:48
  45.4 7.0 %fusion.7 = bf16[512,1536]{1,0:T(8,128)(2,1)} fusion(f32[512,1536]{1,0:T(8,128)} %copy.41, bf16[1536,1536]{1,0:T(8,128)(2,1)} %param.8, bf16[1,512,1536]{2,1,0:T(8,128)(2,1)S(1)} %copy-done.10, f32[512]{0:T(512)S(1)} %fusion.16), kind=kOutput, calls=%fused_computation.18 | convolution fusion | flops 2424569856 | bytes 11012096 | tf_op jit(solution)/shard_map/dot_general | solution.py:106
  52.4 1.7 copy.47
  54.1 3.0 %fusion.27 = f32[32,48,48]{2,1,0:T(8,128)} fusion(bf16[512,32,48]{0,2,1:T(8,128)(2,1)S(1)} %bitcast.69, bf16[512,32,48]{0,2,1:T(8,128)(2,1)} %bitcast.77), kind=kOutput, calls=%fused_computation.46 | convolution fusion | flops 75497472 | bytes 3440640 | tf_op jit(solution)/shard_map/slgi,slgj->igj/dot_general | solution.py:80
  60.0 2.1 copy.52
  64.0 2.2 %pad_maximum_fusion.4 = f32[3,48,1536]{2,1,0:T(8,128)} fusion(f32[1,48,1536]{2,1,0:T(8,128)} %copy.54, f32[1,48,1536]{2,1,0:T(8,128)} %copy.53, f32[1,48,1536]{2,1,0:T(8,128)} %copy.52), kind=kLoop, calls=%fused_computation.31 | loop fusion | flops 442368 | bytes 1769472 | tf_op jit(solution)/shard_map/stack | solution.py:84
  66.3 20.4 %all-reduce.3.cloned.1.call-done = f32[3,48,1536]{2,1,0:T(8,128)} async-done(((f32[3,48,1536]{2,1,0:T(8,128)}), f32[3,48,1536]{2,1,0:T(8,128)}) %all-reduce.3.cloned.1.call-update) | async-done | bytes 884752 | tf_op jit(solution)/shard_map/psum | solution.py:113
  86.8 8.2 %fusion.8 = f32[1536,1536]{1,0:T(8,128)} fusion(bf16[1,512,1536]{2,1,0:T(8,128)(2,1)S(1)} %copy-done.11, f32[1,512,1,1,1,1,1536]{1,6,5,4,3,2,0:T(8,128)} %bitcast.80, f32[512]{0:T(512)S(1)} %fusion.16), kind=kOutput, calls=%fused_computation.23 | convolution fusion | flops 2420637696 | bytes 14157824 | tf_op jit(solution)/shard_map/dot_general | solution.py:116
  96.4 3.7 %collective-permute-start.3 = (bf16[1,64,1536]{2,1,0:T(8,128)(2,1)S(1)}, bf16[1,64,1536]{2,1,0:T(8,128)(2,1)S(1)}, u32[]{:S(2)}, u32[]{:S(2)}) collective-permute-start(bf16[1,64,1536]{2,1,0:T(8,128)(2,1)S(1)} %get-tuple-element.6), channel_id=1, source_target_pairs={{0,2},{2,4},{4,6},{6,8},{8,10},{10,12},{12,14},{1,3},{3,5},{5,7},{... | collective-permute-start | bytes 589832 | tf_op jit(solution)/shard_map/ppermute | solution.py:20
  100.1 1.6 collective-permute-start.2
  101.7 8.4 %fusion.2 = bf16[1,512,1536]{2,1,0:T(8,128)(2,1)} fusion(bf16[1,512,1536]{2,1,0:T(8,128)(2,1)} %param.5, bf16[1536,1536]{1,0:T(8,128)(2,1)} %param.8, f32[512,1536]{1,0:T(8,128)} %copy.41, f32[512]{0:T(512)S(1)} %fusion.16), kind=kOutput, calls=%fused_computation.7 | convolution fusion | flops 2422996992 | bytes 11012096 | tf_op jit(solution)/shard_map/dot_general | solution.py:104
  110.1 2.3 %fusion.24 = f32[32,512,48]{1,2,0:T(8,128)} fusion(bf16[512,32,48]{0,2,1:T(8,128)(2,1)S(1)} %bitcast.72, bf16[48,32,48]{0,2,1:T(8,128)(2,1)S(1)} %bitcast.91), kind=kOutput, calls=%fused_computation.43 | convolution fusion | flops 75497472 | bytes 4866048 | tf_op jit(solution)/shard_map/slgj,igj->slgi/dot_general | solution.py:63
  113.8 2.7 %copy.49 = bf16[1,512,1536]{1,2,0:T(8,128)(2,1)} copy(bf16[1,512,1536]{2,1,0:T(8,128)(2,1)} %get-tuple-element.4) | data formatting | bytes 3145728 | tf_op jit(solution)/shard_map/slice | solution.py:57
  117.2 1.8 fusion.23
  120.2 2.3 %add_add_fusion = f32[32,512,48]{1,2,0:T(8,128)} fusion(f32[32,512,48]{1,2,0:T(8,128)S(1)} %fusion.23, f32[32,512,48]{1,2,0:T(8,128)S(1)} %copy-done.3, bf16[512,32,48]{0,2,1:T(8,128)(2,1)S(1)} %bitcast.85, bf16[48,32,48]{0,2,1:T(8,128)(2,1)S(1)} %bitcast.87), kind=kOutput, calls=%fused_computation.14 | convolution fusion | flops 77070336 | bytes 11157504 | tf_op jit(solution)/shard_map/slgj,igj->slgi/dot_general | solution.py:63
  122.4 2.4 %copy.51 = f32[1,512,1536]{2,1,0:T(8,128)S(1)} copy(f32[1,512,1536]{1,2,0:T(8,128)} %bitcast.81) | data formatting | bytes 6291456 | tf_op jit(solution)/shard_map/reshape | solution.py:66
  124.8 3.0 %add_convert_fusion = bf16[1,512,1536]{2,1,0:T(8,128)(2,1)} fusion(f32[1,512,1536]{2,1,0:T(8,128)S(1)} %copy.51, bf16[1,512,1536]{2,1,0:T(8,128)(2,1)} %param.9, f32[512]{0:T(512)S(1)} %fusion.16), kind=kLoop, calls=%fused_computation.13 | loop fusion | flops 3145728 | bytes 6293504 | tf_op jit(solution)/shard_map/convert_element_type | solution.py:114
  127.8 71.6 %all-reduce.5.cloned.1.call-done = f32[3,48,1536]{2,1,0:T(8,128)} async-done(((f32[3,48,1536]{2,1,0:T(8,128)}), f32[3,48,1536]{2,1,0:T(8,128)}) %all-reduce.5.cloned.1.call-update) | async-done | bytes 884752 | tf_op jit(solution)/shard_map/psum | solution.py:113
  199.4 2.2 broadcast_multiply_fusion
  201.5 10.3 %reduce-scatter.2.cloned.1.call-done = f32[96,1536]{1,0:T(8,128)} async-done(((f32[1536,1536]{1,0:T(8,128)}), f32[96,1536]{1,0:T(8,128)}) %reduce-scatter.2.cloned.1.call-update) | async-done | bytes 589840 | tf_op jit(solution)/shard_map/reduce_scatter | solution.py:115
  211.8 1.9 broadcast_multiply_fusion.1
  (46 shorter events, 14.6 us)
Async XLA Ops:
  8.0 78.7 %all-reduce.3.cloned.1.call-start = ((), (), s32[]{:S(2)}) async-start(), calls=%async_computation.2 | async-start | bytes 1769472 | tf_op jit(solution)/shard_map/psum | solution.py:113
  11.2 18.0 %collective-permute-start.1 = (bf16[1,64,1536]{2,1,0:T(8,128)(2,1)}, bf16[1,64,1536]{2,1,0:T(8,128)(2,1)}, u32[]{:S(2)}, u32[]{:S(2)}) collective-permute-start(bf16[1,64,1536]{2,1,0:T(8,128)(2,1)} %get-tuple-element.10), channel_id=1, source_target_pairs={{2,0},{4,2},{6,4},{8,6},{10,8},{12,10},{14,12},{3,1},{5,3},{7,5},{... | collective-permute-start | bytes 589832 | tf_op jit(solution)/shard_map/ppermute | solution.py:22
  12.5 16.7 %collective-permute-start = (bf16[1,64,1536]{2,1,0:T(8,128)(2,1)}, bf16[1,64,1536]{2,1,0:T(8,128)(2,1)}, u32[]{:S(2)}, u32[]{:S(2)}) collective-permute-start(bf16[1,64,1536]{2,1,0:T(8,128)(2,1)} %get-tuple-element.11), channel_id=1, source_target_pairs={{0,2},{2,4},{4,6},{6,8},{8,10},{10,12},{12,14},{1,3},{3,5},{5,7},{... | collective-permute-start | bytes 589832 | tf_op jit(solution)/shard_map/ppermute | solution.py:20
  36.5 5.3 %copy-start = (bf16[1,512,1536]{1,2,0:T(8,128)(2,1)}, bf16[1,512,1536]{1,2,0:T(8,128)(2,1)S(1)}, u32[]{:S(2)}) copy-start(bf16[1,512,1536]{1,2,0:T(8,128)(2,1)S(1)} %copy.34) | copy-start | bytes 4718596
  36.5 2.1 copy-start.2
  36.5 3.0 %copy-start.4 = (f32[32,512,48]{1,2,0:T(8,128)S(1)}, f32[32,512,48]{1,2,0:T(8,128)}, u32[]{:S(2)}) copy-start(f32[32,512,48]{1,2,0:T(8,128)} %fusion.29) | copy-start | bytes 9437188
  41.7 3.7 %copy-start.10 = (bf16[1,512,1536]{2,1,0:T(8,128)(2,1)S(1)}, bf16[1,512,1536]{2,1,0:T(8,128)(2,1)}, u32[]{:S(2)}) copy-start(bf16[1,512,1536]{2,1,0:T(8,128)(2,1)} %param.9) | copy-start | bytes 4718596
  54.1 4.4 %copy-start.1 = (bf16[1,512,1536]{1,2,0:T(8,128)(2,1)S(1)}, bf16[1,512,1536]{1,2,0:T(8,128)(2,1)}, u32[]{:S(2)}) copy-start(bf16[1,512,1536]{1,2,0:T(8,128)(2,1)} %copy-done) | copy-start | bytes 4718596
  58.5 3.5 %copy-start.9 = (f32[32,48,48]{2,1,0:T(8,128)S(1)}, f32[32,48,48]{2,1,0:T(8,128)}, u32[]{:S(2)}) copy-start(f32[32,48,48]{2,1,0:T(8,128)} %fusion.26) | copy-start | bytes 884740
  58.5 4.5 %copy-start.8 = (f32[32,48,48]{2,1,0:T(8,128)S(1)}, f32[32,48,48]{2,1,0:T(8,128)}, u32[]{:S(2)}) copy-start(f32[32,48,48]{2,1,0:T(8,128)} %fusion.27) | copy-start | bytes 884740
  64.0 22.8 %copy-start.11 = (bf16[1,512,1536]{2,1,0:T(8,128)(2,1)S(1)}, bf16[1,512,1536]{2,1,0:T(8,128)(2,1)}, u32[]{:S(2)}) copy-start(bf16[1,512,1536]{2,1,0:T(8,128)(2,1)} %param.9) | copy-start | bytes 4718596
  66.2 133.1 %all-reduce.5.cloned.1.call-start = ((), (), s32[]{:S(2)}) async-start(), calls=%async_computation.3 | async-start | bytes 1769472 | tf_op jit(solution)/shard_map/psum | solution.py:113
  86.7 125.1 %reduce-scatter.2.cloned.1.call-start = ((), (), s32[]{:S(2)}) async-start(), calls=%async_computation.1 | async-start | bytes 10027008 | tf_op jit(solution)/shard_map/reduce_scatter | solution.py:115
  95.0 1.4 copy-start.5
  96.4 16.0 %collective-permute-start.3 = (bf16[1,64,1536]{2,1,0:T(8,128)(2,1)S(1)}, bf16[1,64,1536]{2,1,0:T(8,128)(2,1)S(1)}, u32[]{:S(2)}, u32[]{:S(2)}) collective-permute-start(bf16[1,64,1536]{2,1,0:T(8,128)(2,1)S(1)} %get-tuple-element.6), channel_id=1, source_target_pairs={{0,2},{2,4},{4,6},{6,8},{8,10},{10,12},{12,14},{1,3},{3,5},{5,7},{... | collective-permute-start | bytes 589832 | tf_op jit(solution)/shard_map/ppermute | solution.py:20
  100.1 10.0 %copy-start.7 = (bf16[1,48,1536]{1,2,0:T(8,128)(2,1)S(1)}, bf16[1,48,1536]{1,2,0:T(8,128)(2,1)}, u32[]{:S(2)}) copy-start(bf16[1,48,1536]{1,2,0:T(8,128)(2,1)} %copy.37) | copy-start | bytes 442372
  100.1 12.3 %collective-permute-start.2 = (bf16[1,64,1536]{2,1,0:T(8,128)(2,1)S(1)}, bf16[1,64,1536]{2,1,0:T(8,128)(2,1)S(1)}, u32[]{:S(2)}, u32[]{:S(2)}) collective-permute-start(bf16[1,64,1536]{2,1,0:T(8,128)(2,1)S(1)} %get-tuple-element.7), channel_id=1, source_target_pairs={{2,0},{4,2},{6,4},{8,6},{10,8},{12,10},{14,12},{3,1},{5,3},{7,5},{... | collective-permute-start | bytes 589832 | tf_op jit(solution)/shard_map/ppermute | solution.py:22
  117.2 2.4 %copy-start.3 = (f32[32,512,48]{1,2,0:T(8,128)S(1)}, f32[32,512,48]{1,2,0:T(8,128)}, u32[]{:S(2)}) copy-start(f32[32,512,48]{1,2,0:T(8,128)} %fusion.24) | copy-start | bytes 9437188
  117.2 2.9 %copy-start.6 = (bf16[1,512,1536]{1,2,0:T(8,128)(2,1)S(1)}, bf16[1,512,1536]{1,2,0:T(8,128)(2,1)}, u32[]{:S(2)}) copy-start(bf16[1,512,1536]{1,2,0:T(8,128)(2,1)} %copy.49) | copy-start | bytes 4718596
Sparse Core Ops, SparseCore 0:
  66.3 20.3 all-reduce.2
  90.6 108.7 all-reduce.4
Sparse Core Ops, SparseCore 1:
  95.1 116.7 reduce-scatter.1
